TPU v7x, 32 devices: a whole 2x2x4 slice. The times are simulated.
32 devices in a mesh: seq: 8 (over z, x), dp: 4 (over y, core).
Axes of the slice: x: 2, y: 2, z: 4, core: 2. Of those that a mesh axis runs over, the one named last changes fastest.
Arguments:
- encoder_out: bfloat16 [4, 2560, 1536], P('dp', 'seq'), may hold values from -0.59765625 to 0.59765625
- out_grad: bfloat16 [4, 2560, 1536], P('dp', 'seq'), may hold values from -12 to 12
- segment_states: bfloat16 [4, 1024, 1536], P('dp', 'seq'), may hold values from -6 to 6
- segment_starts: int32 [4, 1024], P('dp', 'seq'), may hold values from 0 to 320, as said below
- segment_counts: int32 [4, 8], P('dp', 'seq'), may hold values from 32 to 128, as said below
- segment_probs: int32 [4, 1024], P('dp', 'seq'), may hold values from 0 to 65535, as said below
- query_weight: bfloat16 [1536, 1536], P('dp'), may hold values from -0.15625 to 0.15625
- key_weight: bfloat16 [1536, 1536], P('dp'), may hold values from -0.15625 to 0.15625
Outputs:
- x_grad: bfloat16 [4, 2560, 1536], P('dp', 'seq')
- segment_grad: bfloat16 [4, 1024, 1536], P('dp', 'seq')
Inputs may be any that keep to these rules, and one draw needn't show every extreme that they name: `segment_starts`: for block s of sequence b, the entries s * 128 + j with j < segment_counts[b, s] hold distinct increasing local positions below 320 at which segments start; the other entries hold 320. Byte 0 of every sequence starts a segment. `segment_counts`: every sequence has one block with exactly 128 segments and another with exactly a quarter of 128. `segment_probs`: A slot holds 0 exactly when it is past its block's count; slot 0 of every sequence holds 65535.
All inputs are finite; a program needn't handle non-finite values.
Results may differ from a plain program's by a relative error of at most 0.0049.
Values may be sent and summed in bfloat16 or wider, within the bound.
No kernel may reach another device: no remote copies, remote signals or barrier semaphores. Data moves between devices by JAX's collectives and lax.ppermute only.
A program may use at most 64 MiB of HBM per device.

v0:
```python
import jax
import jax.numpy as jnp
from jax import lax
from jax.sharding import PartitionSpec as P

prob_scale = 65536.0
norm_eps = 1e-06
exact = lax.Precision.HIGHEST
contract_last = (((1,), (1,)), ((), ()))
contract_first = (((0,), (0,)), ((), ()))


def shifted(block, axis, distance):
    devices = range(lax.axis_size(axis))
    route = [(i - distance, i) for i in devices if i - distance in devices]
    return lax.ppermute(block, axis, route)


def normalize_grad(vectors, scales, unit_grad):
    inner_prod = jnp.sum(vectors * unit_grad, axis=-1, keepdims=True)
    return scales * unit_grad - scales * scales * scales * inner_prod * vectors


def carry_from(log_keep, vectors, shard_index, from_lower):
    running_log = jnp.cumsum(log_keep)
    before = running_log - log_keep
    shard_order = jnp.arange(log_keep.shape[0])
    if from_lower:
        own_value = lax.dynamic_index_in_dim(before, shard_index, keepdims=False)
        selected = shard_order < shard_index
        log_gap = own_value - running_log
    else:
        own_value = lax.dynamic_index_in_dim(running_log, shard_index, keepdims=False)
        selected = shard_order > shard_index
        log_gap = before - own_value
    factor = jnp.where(selected, jnp.exp(jnp.where(selected, log_gap, 0.0)), 0.0)
    return jnp.dot(factor[None, :], vectors, precision=exact)


def per_device(
    encoder_out,
    out_grad,
    segment_states,
    segment_starts,
    segment_counts,
    segment_probs,
    query_weight,
    key_weight,
):
    token_rows = encoder_out[0]
    grad_rows = out_grad[0]
    token_count = token_rows.shape[0]
    slot_count = segment_states.shape[1]
    shard_index = lax.axis_index("seq")
    full_query, full_key = (
        lax.all_gather(query_weight, "dp", axis=0, tiled=True),
        lax.all_gather(key_weight, "dp", axis=0, tiled=True),
    )
    key_rows = jnp.dot(token_rows, full_key, preferred_element_type=jnp.float32)
    queries = jnp.dot(token_rows, full_query, preferred_element_type=jnp.float32)
    query_scale = lax.rsqrt(jnp.sum(queries * queries, axis=1, keepdims=True) + norm_eps)
    key_scale = lax.rsqrt(jnp.sum(key_rows * key_rows, axis=1, keepdims=True) + norm_eps)
    query_unit = queries * query_scale
    key_unit = key_rows * key_scale
    position = jnp.arange(token_count)
    later_rows = (shard_index > 0) | (position > 0)
    key_before = shifted(key_unit[token_count - 1 :], "seq", 1)
    key_prior = jnp.concatenate([key_before, key_unit[:-1]], axis=0)
    cosine = jnp.sum(query_unit * key_prior, axis=1)
    segment_total = segment_counts[0, 0]
    slot_index = jnp.arange(slot_count)
    slot_used = slot_index < segment_total
    start_pos = segment_starts[0]
    smoothing = jnp.where(slot_used, segment_probs[0].astype(jnp.float32) / prob_scale, 0.0)
    reached = slot_used[None, :] & (start_pos[None, :] <= position[:, None])
    member_id = jnp.sum(reached.astype(jnp.int32), axis=1) - 1
    membership = (member_id[:, None] == slot_index[None, :]).astype(jnp.float32)
    leading = (member_id < 0).astype(jnp.float32)
    starts = jnp.any(slot_used[None, :] & (start_pos[None, :] == position[:, None]), axis=1)
    running = jnp.cumsum(jnp.log(1.0 - smoothing))
    lower = slot_index[None, :] <= slot_index[:, None]
    decay_table = jnp.where(
        lower, jnp.exp(jnp.where(lower, running[:, None] - running[None, :], 0.0)), 0.0
    )
    weighted_states = smoothing[:, None] * segment_states[0].astype(jnp.float32)
    local_state = jnp.dot(decay_table, weighted_states, precision=exact)
    keep_all = jnp.exp(running)
    boundary_prob = jnp.where(later_rows, 0.5 * (1.0 - cosine), 1.0)
    confidence = jnp.where(starts, boundary_prob, 1.0 - boundary_prob)
    weighted_grad = confidence[:, None] * grad_rows
    slot_grad = lax.dot_general(membership, weighted_grad, contract_first, precision=exact)
    lead_grad = jnp.dot(leading[None, :], weighted_grad, precision=exact)
    back_vector = lead_grad + jnp.dot(keep_all[None, :], slot_grad, precision=exact)
    last_log = running[slot_count - 1 :]
    last_state = local_state[slot_count - 1 :]
    summaries = (
        lax.all_gather(last_log, "seq", axis=0, tiled=True),
        lax.all_gather(last_state, "seq", axis=0, tiled=True),
        lax.all_gather(last_log, "seq", axis=0, tiled=True),
        lax.all_gather(back_vector, "seq", axis=0, tiled=True),
    )
    state_in = carry_from(summaries[0], summaries[1], shard_index, True)
    grad_in = carry_from(summaries[2], summaries[3], shard_index, False)
    smoothed = local_state + keep_all[:, None] * state_in
    picked = jnp.dot(membership, smoothed, precision=exact) + leading[:, None] * state_in
    conf_grad = jnp.sum(grad_rows * picked, axis=1)
    cos_grad = jnp.where(later_rows, jnp.where(starts, -0.5 * conf_grad, 0.5 * conf_grad), 0.0)
    reach_end = jnp.exp(running[slot_count - 1] - running)
    state_grad = (
        lax.dot_general(decay_table, slot_grad, contract_first, precision=exact)
        + reach_end[:, None] * grad_in
    )
    segment_grad = (smoothing[:, None] * state_grad).astype(jnp.bfloat16)
    unit_q_grad = cos_grad[:, None] * key_prior
    prior_grad = cos_grad[:, None] * query_unit
    query_grad = normalize_grad(queries, query_scale, unit_q_grad).astype(jnp.bfloat16)
    from_next = shifted(prior_grad[:1], "seq", -1)
    unit_k_grad = jnp.concatenate([prior_grad[1:], from_next], axis=0)
    key_grad = normalize_grad(key_rows, key_scale, unit_k_grad).astype(jnp.bfloat16)
    x_grad = lax.dot_general(
        query_grad, full_query, contract_last, preferred_element_type=jnp.float32
    )
    x_grad = x_grad + lax.dot_general(
        key_grad, full_key, contract_last, preferred_element_type=jnp.float32
    )
    return (x_grad.astype(jnp.bfloat16)[None], segment_grad[None])


def solution(mesh):
    placed = (
        P("dp", "seq", None),
        P("dp", "seq", None),
        P("dp", "seq", None),
        P("dp", "seq"),
        P("dp", "seq"),
        P("dp", "seq"),
        P("dp", None),
        P("dp", None),
    )
    return jax.shard_map(
        per_device,
        mesh=mesh,
        in_specs=placed,
        out_specs=(P("dp", "seq", None), P("dp", "seq", None)),
        check_vma=False,
    )
```

profile of v0, /device:TPU:0, one launch (start us, length us, event | category | flops | bytes accessed | tf_op | source)
XLA Modules:
  0.0 151.8 jit_solution(7152754689850499982)
XLA Ops:
  7.3 0.7 all-gather.7.cloned.1.call-update
  8.0 0.7 all-gather.9.cloned.1.call-update
  10.8 1.3 bitcast_dynamic-update-slice_fusion
  12.1 23.1 %all-reduce = f32[8]{0:T(128)S(1)} all-reduce(f32[8]{0:T(128)S(1)} %bitcast_dynamic-update-slice_fusion), channel_id=2, replica_groups=mesh['seq'=8,'dp'=4] {'seq'}, use_global_device_ids=true, to_apply=%add | all-reduce | flops 8 | bytes 64
  36.1 0.9 fusion.24
  37.0 30.7 %all-gather.2 = f32[8,1,1536]{2,1,0:T(1,128)S(1)} all-gather(f32[1,1,1536]{2,1,0:T(1,128)S(1)} %slice_bitcast_fusion), channel_id=1, replica_groups=mesh['seq'=8,'dp'=4] {'seq'}, dimensions={0}, use_global_device_ids=true | all-gather | bytes 55296 | tf_op jit(solution)/shard_map/all_gather | solution.py:98
  67.7 0.8 convolution_reduce_fusion.2
  68.9 0.6 subtract_exponential_fusion
  69.6 1.5 fusion.8
  71.1 4.2 %multiply_reduce_fusion.4 = (f32[320]{0:T(512)S(1)}, f32[320,1536]{1,0:T(8,128)S(1)}) fusion(bf16[1536,1536]{1,0:T(8,128)(2,1)} %all-gather.7.cloned.1.call-done, bf16[1,320,1536]{2,1,0:T(8,128)(2,1)S(1)} %copy-done), kind=kOutput, calls=%fused_computation.20 | convolution fusion | flops 1510932224 | bytes 7668992 | tf_op jit(solution)/shard_map/dot_general | solution.py:60
  75.5 1.3 collective-permute-start.1
  76.8 1.4 slice.33
  78.3 10.6 %all-gather.9.cloned.1.call-done = bf16[1536,1536]{1,0:T(8,128)(2,1)} async-done(((bf16[384,1536]{1,0:T(8,128)(2,1)}), bf16[1536,1536]{1,0:T(8,128)(2,1)}) %all-gather.9.cloned.1.call-update) | async-done | bytes 4718608 | tf_op jit(solution)/shard_map/all_gather | solution.py:57
  88.9 4.8 %multiply_reduce_fusion.1 = (f32[320]{0:T(512)S(1)}, f32[320]{0:T(512)S(1)}, f32[320,1536]{1,0:T(8,128)S(1)}) fusion(f32[1,1536]{1,0:T(1,128)S(1)} %collective-permute-done.1, f32[319,1536]{1,0:T(8,128)} %slice.33, bf16[1536,1536]{1,0:T(8,128)(2,1)} %all-gather.9.cloned.1.call-done, bf16[1,320,1536]{2,1,0:T(8,128)(2,1)S(1)} %copy-done), kind=kOutput, calls=%fused_computation.16 | convolution fusion | flops 1512406528 | bytes 9636352 | tf_op jit(solution)/shard_map/dot_general | solution.py:59
  93.9 3.4 %collective-permute-start = (f32[1,1536]{1,0:T(1,128)S(1)}, f32[1,1536]{1,0:T(1,128)S(1)}, u32[]{:S(2)}, u32[]{:S(2)}) collective-permute-start(f32[1,1536]{1,0:T(1,128)S(1)} %slice.31), channel_id=1, source_target_pairs={{0,4},{4,8},{8,12},{12,16},{16,20},{20,24},{24,28},{1,5},{5,9},{9,... | collective-permute-start | bytes 18440 | tf_op jit(solution)/shard_map/ppermute | solution.py:16
  97.9 0.7 collective-permute-done
  98.7 0.8 multiply_reduce_fusion
  99.9 1.2 fusion.7
  101.1 0.9 fusion.9
  102.6 32.6 %all-gather.3 = f32[8,1,1536]{2,1,0:T(1,128)S(1)} all-gather(f32[1,1,1536]{2,1,0:T(1,128)S(1)} %reshape.174), channel_id=3, replica_groups=mesh['seq'=8,'dp'=4] {'seq'}, dimensions={0}, use_global_device_ids=true | all-gather | bytes 55296 | tf_op jit(solution)/shard_map/all_gather | solution.py:100
  135.2 0.8 convolution_reduce_fusion.1
  136.0 1.7 %fusion.5 = bf16[1,128,1536]{2,1,0:T(8,128)(2,1)} fusion(f32[128,1536]{1,0:T(8,128)S(1)} %fusion.7, f32[1536]{0:T(1024)S(1)} %convolution_reduce_fusion.1, f32[128]{0:T(128)S(1)} %get-tuple-element.10, f32[128]{0:T(128)S(1)} %bitcast_select_fusion, f32[128]{0:T(128)S(1)} %reduce), kind=kOutput, calls=%fused_computation.9 | convolution fusion | flops 302841856 | bytes 1187328 | tf_op jit(solution)/shard_map/dot_general | solution.py:110
  137.7 4.3 %fusion.10 = f32[320,1536]{1,0:T(8,128)S(1)} fusion(bf16[1536,1536]{1,0:T(8,128)(2,1)} %all-gather.7.cloned.1.call-done, f32[320,1536]{1,0:T(8,128)S(1)} %get-tuple-element.13, f32[319,1536]{1,0:T(8,128)S(1)} %bitcast.85, f32[1,1536]{1,0:T(1,128)S(1)} %collective-permute-done, f32[320]{0:T(512)S(1)} %get-tuple-element.16, f32[320]{0:T(512)S(1)} %select_select_fusion, ...), kind=kOutput, calls=%fused_computation.27 | convolution fusion | flops 1512898560 | bytes 10620672 | tf_op jit(solution)/shard_map/dot_general | solution.py:120
  142.1 2.9 %fusion.2 = bf16[1,320,1536]{2,1,0:T(8,128)(2,1)} fusion(f32[320,1536]{1,0:T(8,128)S(1)} %fusion.10, bf16[1536,1536]{1,0:T(8,128)(2,1)S(1)} %bitcast.89, f32[320,1536]{1,0:T(8,128)S(1)} %get-tuple-element.14, f32[1,1536]{1,0:T(1,128)S(1)} %collective-permute-done.1, f32[319,1536]{1,0:T(8,128)S(1)} %copy-done.3, f32[320]{0:T(512)S(1)} %get-tuple-element.8, ...), kind=kOutput, calls=%fused_computation.4 | convolution fusion | flops 1513390080 | bytes 11602432 | tf_op jit(solution)/shard_map/dot_general | solution.py:123
  (55 shorter events, 4.8 us)
Async XLA Ops:
  7.2 63.9 %copy-start = (bf16[1,320,1536]{2,1,0:T(8,128)(2,1)S(1)}, bf16[1,320,1536]{2,1,0:T(8,128)(2,1)}, u32[]{:S(2)}) copy-start(bf16[1,320,1536]{2,1,0:T(8,128)(2,1)} %param.8) | copy-start | bytes 2949124
  7.2 3.1 %copy-start.7 = (u32[32]{0:T(128)S(1)}, u32[32]{0:T(128)}, u32[]{:S(2)}) copy-start(u32[32]{0:T(128)} %constant.53) | copy-start | bytes 388
  7.2 2.2 %copy-start.6 = (s32[1,128]{1,0:T(1,128)S(1)}, s32[1,128]{1,0:T(1,128)}, u32[]{:S(2)}) copy-start(s32[1,128]{1,0:T(1,128)} %param.13) | copy-start | bytes 1540
  7.2 28.9 %copy-start.4 = (bf16[1,128,1536]{2,1,0:T(8,128)(2,1)S(1)}, bf16[1,128,1536]{2,1,0:T(8,128)(2,1)}, u32[]{:S(2)}) copy-start(bf16[1,128,1536]{2,1,0:T(8,128)(2,1)} %param.10) | copy-start | bytes 1179652
  7.2 61.4 %copy-start.5 = (s32[1,128]{1,0:T(1,128)S(1)}, s32[1,128]{1,0:T(1,128)}, u32[]{:S(2)}) copy-start(s32[1,128]{1,0:T(1,128)} %param.11) | copy-start | bytes 1540
  7.2 62.3 %copy-start.1 = (bf16[1,320,1536]{2,1,0:T(8,128)(2,1)S(1)}, bf16[1,320,1536]{2,1,0:T(8,128)(2,1)}, u32[]{:S(2)}) copy-start(bf16[1,320,1536]{2,1,0:T(8,128)(2,1)} %param.9) | copy-start | bytes 2949124
  7.2 63.8 %all-gather.7.cloned.1.call-start = ((), (), s32[]{:S(2)}) async-start(), calls=%async_computation | async-start | bytes 5898240 | tf_op jit(solution)/shard_map/all_gather | solution.py:56
  8.0 80.9 %all-gather.9.cloned.1.call-start = ((), (), s32[]{:S(2)}) async-start(), calls=%async_computation.1 | async-start | bytes 5898240 | tf_op jit(solution)/shard_map/all_gather | solution.py:57
  75.5 13.4 %collective-permute-start.1 = (f32[1,1536]{1,0:T(1,128)S(1)}, f32[1,1536]{1,0:T(1,128)S(1)}, u32[]{:S(2)}, u32[]{:S(2)}) collective-permute-start(f32[1,1536]{1,0:T(1,128)S(1)} %slice.34), channel_id=1, source_target_pairs={{4,0},{8,4},{12,8},{16,12},{20,16},{24,20},{28,24},{5,1},{9,5},{13... | collective-permute-start | bytes 18440 | tf_op jit(solution)/shard_map/ppermute | solution.py:16
  93.9 4.7 %collective-permute-start = (f32[1,1536]{1,0:T(1,128)S(1)}, f32[1,1536]{1,0:T(1,128)S(1)}, u32[]{:S(2)}, u32[]{:S(2)}) collective-permute-start(f32[1,1536]{1,0:T(1,128)S(1)} %slice.31), channel_id=1, source_target_pairs={{0,4},{4,8},{8,12},{12,16},{16,20},{20,24},{24,28},{1,5},{5,9},{9,... | collective-permute-start | bytes 18440 | tf_op jit(solution)/shard_map/ppermute | solution.py:16
  98.7 1.2 copy-start.2
  136.0 6.0 %slice-start = ((s8[4718592]{0:T(1024)(128)(4,1)}), s8[4194304]{0:T(1024)(128)(4,1)S(1)}, s32[]{:S(2)}) async-start(s8[4718592]{0:T(1024)(128)(4,1)} %bitcast.88), calls=%async_computation.2 | async-start | bytes 8388608
  137.7 4.4 %copy-start.3 = (f32[319,1536]{1,0:T(8,128)S(1)}, f32[319,1536]{1,0:T(8,128)}, u32[]{:S(2)}) copy-start(f32[319,1536]{1,0:T(8,128)} %slice.33) | copy-start | bytes 5879812
  137.7 4.4 %slice-start.1 = ((s8[4718592]{0:T(1024)(128)(4,1)}), s8[524288]{0:T(1024)(128)(4,1)S(1)}, s32[]{:S(2)}) async-start(s8[4718592]{0:T(1024)(128)(4,1)} %bitcast.88), calls=%async_computation.3 | async-start | bytes 1048576
Sparse Core Ops, SparseCore 0:
  9.6 40.1 all-gather.6
  51.4 37.4 all-gather.8
where the time goes:
time: 152 us
  blocking collectives  86.4 us (57%)
  matrix products  24.5 us (16%)
  between operations  15 us (10%)
  waiting for transfers between devices  12.7 us (8%)
  local copies, waits for them, and re-layouts  5.63 us (4%)
  starting transfers between devices  4.76 us (3%)
  other arithmetic  2.75 us (2%)
    all_gather x1, blocking collectives, per_device(): lax.all_gather(back_vector, 'seq', axis=0, tiled=True)  32.6 us
    all_gather x1, blocking collectives, per_device(): lax.all_gather(last_state, 'seq', axis=0, tiled=True)  30.7 us
    unnamed x1, blocking collectives  23.1 us
    all_gather x1, waiting for transfers between devices, per_device(): lax.all_gather(key_weight, 'dp', axis=0, tiled=True)  10.6 us
    dot_general x1, matrix products, per_device(): key_rows = jnp.dot(token_rows, full_key, preferred_element_type=jnp.float32)  4.83 us
    ppermute x2, starting transfers between devices, shifted(): return lax.ppermute(block, axis, route)  4.68 us
    dot_general x1, matrix products, per_device(): lax.dot_general(query_grad, full_query, contract_last, preferred_element_...  4.34 us
    dot_general x1, matrix products, per_device(): jnp.dot(token_rows, full_query, preferred_element_type=jnp.float32)  4.17 us
  transfers between devices with their start and end apart: 4, of which 2 were waited for; matrix products, arithmetic and copies ran while one was open for 9% of the time, Pallas kernels for 0%

commit v1 on v0

--- a/solution.py
+++ b/solution.py
@@ -8,6 +8,27 @@
 exact = lax.Precision.HIGHEST
 contract_last = (((1,), (1,)), ((), ()))
 contract_first = (((0,), (0,)), ((), ()))
+
+
+def collect(x, axis, dim):
+    devices, position, span = (lax.axis_size(axis), lax.axis_index(axis), x.shape[dim])
+    ahead = [(i, (i + 1) % devices) for i in range(devices)]
+    backward = [(i, (i - 1) % devices) for i in range(devices)]
+    filled = jnp.zeros((*x.shape[:dim], devices * span, *x.shape[dim + 1 :]), x.dtype)
+    filled = lax.dynamic_update_slice_in_dim(filled, x, position * span, axis=dim)
+    from_left = from_right = x
+    middle = devices // 2
+    for hop in range(1, middle + 1):
+        from_left = lax.ppermute(from_left, axis, ahead)
+        filled = lax.dynamic_update_slice_in_dim(
+            filled, from_left, (position - hop) % devices * span, axis=dim
+        )
+        if hop < devices - middle:
+            from_right = lax.ppermute(from_right, axis, backward)
+            filled = lax.dynamic_update_slice_in_dim(
+                filled, from_right, (position + hop) % devices * span, axis=dim
+            )
+    return filled
 
 
 def shifted(block, axis, distance):
@@ -54,7 +75,7 @@
     shard_index = lax.axis_index("seq")
     full_query, full_key = (
         lax.all_gather(query_weight, "dp", axis=0, tiled=True),
-        lax.all_gather(key_weight, "dp", axis=0, tiled=True),
+        collect(key_weight, "dp", 0),
     )
     key_rows = jnp.dot(token_rows, full_key, preferred_element_type=jnp.float32)
     queries = jnp.dot(token_rows, full_query, preferred_element_type=jnp.float32)

time: 152 us -> 158 us (1.039)
  local copies, waits for them, and re-layouts: 5.63 us -> 14.9 us
  waiting for transfers between devices: 12.7 us -> 7.87 us
    all_gather x1 -> x0, waiting for transfers between devices: 10.6 us -> none  [per_device(): lax.all_gather(key_weight, 'dp', axis=0, tiled=True)]
    dynamic_update_slice x0 -> x4, local copies, waits for them, and re-layouts: none -> 7.05 us  [the longest x2 3.55 us: collect(): lax.dynamic_update_slice_in_dim(filled, from_left, (position - hop) % dev...]
    ppermute x0 -> x3, waiting for transfers between devices: none -> 6.45 us  [the longest x2 6.45 us: collect(): from_left = lax.ppermute(from_left, axis, ahead)]
    ppermute x0 -> x3, starting transfers between devices: none -> 2.53 us  [the longest x1 2.02 us: collect(): from_right = lax.ppermute(from_right, axis, backward)]
    dot_general x1, matrix products: 4.34 us -> 1.84 us  [per_device(): lax.dot_general(query_grad, full_query, contract_last, preferred_element_...]
    broadcast_in_dim x0 -> x1, local copies, waits for them, and re-layouts: none -> 2.48 us  [collect(): jnp.zeros((*x.shape[:dim], devices * span, *x.shape[dim + 1:]), x.dtype)]
    dot_general x1, matrix products: 2.85 us -> 5.03 us  [per_device(): lax.dot_general(key_grad, full_key, contract_last, preferred_element_type...]
    ppermute x2, starting transfers between devices: 4.68 us -> 2.85 us  [shifted(): return lax.ppermute(block, axis, route)]
  transfers between devices with their start and end apart: 4 -> 6, of which waited for: 2 -> 2; matrix products, arithmetic and copies ran while one was open for 9% -> 17% of each run, Pallas kernels for 0% -> 0%
where the time goes in v1:
time: 158 us
  blocking collectives  85 us (54%)
  matrix products  25.6 us (16%)
  between operations  15 us (9%)
  local copies, waits for them, and re-layouts  14.9 us (9%)
  waiting for transfers between devices  7.87 us (5%)
  starting transfers between devices  5.41 us (3%)
  other arithmetic  4.01 us (3%)
    all_gather x1, blocking collectives, per_device(): lax.all_gather(back_vector, 'seq', axis=0, tiled=True)  31.9 us
    all_gather x1, blocking collectives, per_device(): lax.all_gather(last_state, 'seq', axis=0, tiled=True)  30.7 us
    unnamed x1, blocking collectives  22.4 us
    ppermute x2, waiting for transfers between devices, collect(): from_left = lax.ppermute(from_left, axis, ahead)  6.45 us
    dot_general x1, matrix products, per_device(): lax.dot_general(key_grad, full_key, contract_last, preferred_element_type...  5.03 us
    dot_general x1, matrix products, per_device(): key_rows = jnp.dot(token_rows, full_key, preferred_element_type=jnp.float32)  4.18 us
    dot_general x1, matrix products, per_device(): jnp.dot(token_rows, full_query, preferred_element_type=jnp.float32)  4.12 us
    dynamic_update_slice x2, local copies, waits for them, and re-layouts, collect(): lax.dynamic_update_slice_in_dim(filled, from_left, (position - hop) % dev...  3.55 us
  transfers between devices with their start and end apart: 6, of which 2 were waited for; matrix products, arithmetic and copies ran while one was open for 17% of the time, Pallas kernels for 0%

profile of v1, /device:TPU:0, one launch (start us, length us, event | category | flops | bytes accessed | tf_op | source)
XLA Modules:
  0.0 157.8 jit_solution(8674461264736432324)
XLA Ops:
  10.5 1.2 dynamic-slice.2
  11.8 1.2 bitcast_dynamic-update-slice_fusion
  13.0 2.0 %collective-permute-start.1 = (bf16[384,1536]{1,0:T(8,128)(2,1)}, bf16[384,1536]{1,0:T(8,128)(2,1)}, u32[]{:S(2)}, u32[]{:S(2)}) collective-permute-start(bf16[384,1536]{1,0:T(8,128)(2,1)} %param.15), channel_id=1, source_target_pairs={{0,3},{1,0},{2,1},{3,2},{4,7},{5,4},{6,5},{7,6},{8,11},{9,8},{10,9... | collective-permute-start | bytes 3538952 | tf_op jit(solution)/shard_map/ppermute | solution.py:27
  15.0 22.4 %all-reduce = f32[8]{0:T(128)S(1)} all-reduce(f32[8]{0:T(128)S(1)} %bitcast_dynamic-update-slice_fusion), channel_id=2, replica_groups=mesh['seq'=8,'dp'=4] {'seq'}, use_global_device_ids=true, to_apply=%add | all-reduce | flops 8 | bytes 64
  39.0 1.9 %fusion.23 = f32[128,1536]{1,0:T(8,128)S(1)} fusion(bf16[1,128,1536]{2,1,0:T(8,128)(2,1)} %param.10, f32[128]{0:T(128)S(1)} %bitcast_select_fusion, f32[128]{0:T(128)S(1)} %reduce), kind=kOutput, calls=%fused_computation.43 | convolution fusion | flops 302448640 | bytes 1180672 | tf_op jit(solution)/shard_map/dot_general | solution.py:107
  40.9 0.9 copy-done.3
  41.8 30.7 %all-gather.2 = f32[8,1,1536]{2,1,0:T(1,128)S(1)} all-gather(f32[1,1,1536]{2,1,0:T(1,128)S(1)} %slice_bitcast_fusion), channel_id=1, replica_groups=mesh['seq'=8,'dp'=4] {'seq'}, dimensions={0}, use_global_device_ids=true | all-gather | bytes 55296 | tf_op jit(solution)/shard_map/all_gather | solution.py:119
  74.3 2.6 %fusion.8 = f32[320]{0:T(512)S(1)} fusion(bf16[1,320,1536]{2,1,0:T(8,128)(2,1)S(1)} %copy-done.1, f32[1536]{0:T(1024)S(1)} %convolution_reduce_fusion.2, f32[320]{0:T(512)S(1)} %get-tuple-element.6, f32[128,1536]{1,0:T(8,128)} %copy-done.3, f32[128]{0:T(128)S(1)} %get-tuple-element.11, s32[320]{0:T(512)S(1)} %broadcast_add_fusion), kind=kOutput, calls=%fused_computation.23 | convolution fusion | flops 757866176 | bytes 1779968 | tf_op jit(solution)/shard_map/dot_general | solution.py:126
  76.9 2.5 %broadcast_in_dim.68 = bf16[1536,1536]{1,0:T(8,128)(2,1)} broadcast(bf16[]{:T(256)} %constant.71.clone.1), dimensions={} | broadcast | bytes 4718594 | tf_op jit(solution)/shard_map/broadcast_in_dim | solution.py:17
  79.4 1.1 constant_dynamic-update-slice_fusion.3
  80.5 1.2 constant_dynamic-update-slice_fusion.2
  81.7 2.4 %constant_dynamic-update-slice_fusion.1 = bf16[1536,1536]{1,0:T(8,128)(2,1)} fusion(bf16[1536,1536]{1,0:T(8,128)(2,1)} %constant_dynamic-update-slice_fusion.2, bf16[384,1536]{1,0:T(8,128)(2,1)} %collective-permute-done.1, s32[]{:T(128)S(6)} %select_n.115), kind=kLoop, calls=%fused_computation.86 | loop fusion | bytes 2359300 | tf_op jit(solution)/shard_map/dynamic_update_slice | solution.py:28
  84.1 4.1 %multiply_reduce_fusion.4 = (f32[320]{0:T(512)S(1)}, f32[320,1536]{1,0:T(8,128)S(1)}) fusion(bf16[1536,1536]{1,0:T(8,128)(2,1)} %all-gather.6.cloned.1.call-done, bf16[1,320,1536]{2,1,0:T(8,128)(2,1)S(1)} %copy-done), kind=kOutput, calls=%fused_computation.21 | convolution fusion | flops 1510932224 | bytes 7668992 | tf_op jit(solution)/shard_map/dot_general | solution.py:81
  88.5 1.3 collective-permute-start.4
  89.8 6.4 %collective-permute-done.2 = bf16[384,1536]{1,0:T(8,128)(2,1)} collective-permute-done((bf16[384,1536]{1,0:T(8,128)(2,1)S(1)}, bf16[384,1536]{1,0:T(8,128)(2,1)}, u32[]{:S(2)}, u32[]{:S(2)}) %collective-permute-start.2) | collective-permute-done | bytes 1179680 | tf_op jit(solution)/shard_map/ppermute | solution.py:22
  96.2 2.4 %constant_dynamic-update-slice_fusion = bf16[1536,1536]{1,0:T(8,128)(2,1)} fusion(bf16[1536,1536]{1,0:T(8,128)(2,1)} %constant_dynamic-update-slice_fusion.1, bf16[384,1536]{1,0:T(8,128)(2,1)} %collective-permute-done.2, s32[]{:T(128)S(6)} %select_n.117), kind=kLoop, calls=%fused_computation.85 | loop fusion | bytes 2359300 | tf_op jit(solution)/shard_map/dynamic_update_slice | solution.py:23
  98.8 4.2 %multiply_reduce_fusion.1 = (f32[320]{0:T(512)S(1)}, f32[320]{0:T(512)S(1)}, f32[320,1536]{1,0:T(8,128)S(1)}) fusion(f32[1,1536]{1,0:T(1,128)S(1)} %collective-permute-done.4, f32[319,1536]{1,0:T(8,128)S(1)} %slice.33, bf16[1536,1536]{1,0:T(8,128)(2,1)} %constant_dynamic-update-slice_fusion, bf16[1,320,1536]{2,1,0:T(8,128)(2,1)S(1)} %copy-done), kind=kOutput, calls=%fused_computation.17 | convolution fusion | flops 1512406528 | bytes 9636352 | tf_op jit(solution)/shard_map/dot_general | solution.py:80
  103.2 1.6 collective-permute-start.3
  107.0 1.2 fusion.7
  108.7 0.9 fusion.9
  109.7 31.9 %all-gather.3 = f32[8,1,1536]{2,1,0:T(1,128)S(1)} all-gather(f32[1,1,1536]{2,1,0:T(1,128)S(1)} %reshape.174), channel_id=3, replica_groups=mesh['seq'=8,'dp'=4] {'seq'}, dimensions={0}, use_global_device_ids=true | all-gather | bytes 55296 | tf_op jit(solution)/shard_map/all_gather | solution.py:121
  142.4 1.7 %fusion.5 = bf16[1,128,1536]{2,1,0:T(8,128)(2,1)} fusion(f32[128,1536]{1,0:T(8,128)S(1)} %fusion.7, f32[1536]{0:T(1024)S(1)} %convolution_reduce_fusion.1, f32[128]{0:T(128)S(1)} %get-tuple-element.10, f32[128]{0:T(128)S(1)} %bitcast_select_fusion, f32[128]{0:T(128)S(1)} %reduce), kind=kOutput, calls=%fused_computation.10 | convolution fusion | flops 302841856 | bytes 1187328 | tf_op jit(solution)/shard_map/dot_general | solution.py:131
  144.1 1.8 %fusion.10 = f32[320,1536]{1,0:T(8,128)S(1)} fusion(bf16[1536,1536]{1,0:T(8,128)(2,1)S(1)} %bitcast.91, f32[320,1536]{1,0:T(8,128)S(1)} %get-tuple-element.13, f32[319,1536]{1,0:T(8,128)S(1)} %bitcast.87, f32[1,1536]{1,0:T(1,128)S(1)} %collective-permute-done.3, f32[320]{0:T(512)S(1)} %get-tuple-element.16, f32[320]{0:T(512)S(1)} %select_select_fusion, ...), kind=kOutput, calls=%fused_computation.28 | convolution fusion | flops 1512898560 | bytes 10620672 | tf_op jit(solution)/shard_map/dot_general | solution.py:141
  146.0 5.0 %fusion.2 = bf16[1,320,1536]{2,1,0:T(8,128)(2,1)} fusion(f32[320,1536]{1,0:T(8,128)S(1)} %fusion.10, bf16[1536,1536]{1,0:T(8,128)(2,1)} %constant_dynamic-update-slice_fusion, f32[320,1536]{1,0:T(8,128)S(1)} %get-tuple-element.14, f32[1,1536]{1,0:T(1,128)S(1)} %collective-permute-done.4, f32[319,1536]{1,0:T(8,128)S(1)} %slice.33, ...), kind=kOutput, calls=%fused_computation.5 | convolution fusion | flops 1513390080 | bytes 11602432 | tf_op jit(solution)/shard_map/dot_general | solution.py:144
  (57 shorter events, 10.2 us)
Async XLA Ops:
  7.2 76.9 %copy-start = (bf16[1,320,1536]{2,1,0:T(8,128)(2,1)S(1)}, bf16[1,320,1536]{2,1,0:T(8,128)(2,1)}, u32[]{:S(2)}) copy-start(bf16[1,320,1536]{2,1,0:T(8,128)(2,1)} %param.8) | copy-start | bytes 2949124
  7.2 65.3 %copy-start.4 = (s32[1,128]{1,0:T(1,128)S(1)}, s32[1,128]{1,0:T(1,128)}, u32[]{:S(2)}) copy-start(s32[1,128]{1,0:T(1,128)} %param.11) | copy-start | bytes 1540
  7.2 67.1 %copy-start.1 = (bf16[1,320,1536]{2,1,0:T(8,128)(2,1)S(1)}, bf16[1,320,1536]{2,1,0:T(8,128)(2,1)}, u32[]{:S(2)}) copy-start(bf16[1,320,1536]{2,1,0:T(8,128)(2,1)} %param.9) | copy-start | bytes 2949124
  7.2 76.9 %all-gather.6.cloned.1.call-start = ((), (), s32[]{:S(2)}) async-start(), calls=%async_computation | async-start | bytes 5898240 | tf_op jit(solution)/shard_map/all_gather | solution.py:77
  7.9 72.6 %collective-permute-start = (bf16[384,1536]{1,0:T(8,128)(2,1)}, bf16[384,1536]{1,0:T(8,128)(2,1)S(1)}, u32[]{:S(2)}, u32[]{:S(2)}) collective-permute-start(bf16[384,1536]{1,0:T(8,128)(2,1)} %param.15), channel_id=1, source_target_pairs={{0,1},{1,2},{2,3},{3,0},{4,5},{5,6},{6,7},{7,4},{8,9},{9,10},{10,1... | collective-permute-start | bytes 3538952 | tf_op jit(solution)/shard_map/ppermute | solution.py:22
  13.0 68.7 %collective-permute-start.1 = (bf16[384,1536]{1,0:T(8,128)(2,1)}, bf16[384,1536]{1,0:T(8,128)(2,1)}, u32[]{:S(2)}, u32[]{:S(2)}) collective-permute-start(bf16[384,1536]{1,0:T(8,128)(2,1)} %param.15), channel_id=1, source_target_pairs={{0,3},{1,0},{2,1},{3,2},{4,7},{5,4},{6,5},{7,6},{8,11},{9,8},{10,9... | collective-permute-start | bytes 3538952 | tf_op jit(solution)/shard_map/ppermute | solution.py:27
  40.9 0.9 copy-start.3
  76.9 2.5 %copy-start.2 = (bf16[384,1536]{1,0:T(8,128)(2,1)S(1)}, bf16[384,1536]{1,0:T(8,128)(2,1)}, u32[]{:S(2)}) copy-start(bf16[384,1536]{1,0:T(8,128)(2,1)} %param.15) | copy-start | bytes 3538948
  80.5 15.7 %collective-permute-start.2 = (bf16[384,1536]{1,0:T(8,128)(2,1)S(1)}, bf16[384,1536]{1,0:T(8,128)(2,1)}, u32[]{:S(2)}, u32[]{:S(2)}) collective-permute-start(bf16[384,1536]{1,0:T(8,128)(2,1)S(1)} %collective-permute-done), channel_id=1, source_target_pairs={{0,1},{1,2},{2,3},{3,0},{4,5},{5,6},{6,7},{7,4},{8,9},{9,10},{10,1... | collective-permute-start | bytes 3538952 | tf_op jit(solution)/shard_map/ppermute | solution.py:22
  88.5 10.3 %collective-permute-start.4 = (f32[1,1536]{1,0:T(1,128)S(1)}, f32[1,1536]{1,0:T(1,128)S(1)}, u32[]{:S(2)}, u32[]{:S(2)}) collective-permute-start(f32[1,1536]{1,0:T(1,128)S(1)} %slice.34), channel_id=1, source_target_pairs={{4,0},{8,4},{12,8},{16,12},{20,16},{24,20},{28,24},{5,1},{9,5},{13... | collective-permute-start | bytes 18440 | tf_op jit(solution)/shard_map/ppermute | solution.py:37
  103.0 41.1 %slice-start = ((s8[4718592]{0:T(1024)(128)(4,1)}), s8[4194304]{0:T(1024)(128)(4,1)S(1)}, s32[]{:S(2)}) async-start(s8[4718592]{0:T(1024)(128)(4,1)} %bitcast.90), calls=%async_computation.1 | async-start | bytes 8388608
  103.2 2.9 %collective-permute-start.3 = (f32[1,1536]{1,0:T(1,128)S(1)}, f32[1,1536]{1,0:T(1,128)S(1)}, u32[]{:S(2)}, u32[]{:S(2)}) collective-permute-start(f32[1,1536]{1,0:T(1,128)S(1)} %slice.31), channel_id=1, source_target_pairs={{0,4},{4,8},{8,12},{12,16},{16,20},{20,24},{24,28},{1,5},{5,9},{9,... | collective-permute-start | bytes 18440 | tf_op jit(solution)/shard_map/ppermute | solution.py:37
  106.1 38.0 %slice-start.1 = ((s8[4718592]{0:T(1024)(128)(4,1)}), s8[524288]{0:T(1024)(128)(4,1)S(1)}, s32[]{:S(2)}) async-start(s8[4718592]{0:T(1024)(128)(4,1)} %bitcast.90), calls=%async_computation.2 | async-start | bytes 1048576
Sparse Core Ops, SparseCore 0:
  9.6 54.4 all-gather.5
